TPU v7x, 512 devices: a whole 4x8x8 slice. The times are simulated.
512 devices in a mesh: space: 64 (over z_lo, y, core), chan: 8 (over x, z_hi).
Axes of the slice: x: 4, y: 8, z: 8 (z_hi: 2, z_lo: 4; z = z_hi * 4 + z_lo), core: 2. Of those that a mesh axis runs over, the one named last changes fastest.
Arguments:
- features: bfloat16 [1, 128, 128, 2048], P(None, 'chan', 'space'), may hold values from -6 to 6
- top_map: int32 [64, 2048], P('space'), may hold values from 0 to 2048, as said below
- bottom_map: int32 [64, 2048], P('space'), may hold values from 0 to 2048, as said below
- first_weight: bfloat16 [128, 3, 3, 128], P('chan'), may hold values from -0.1875 to 0.1875
- first_bias: float32 [128], P('chan'), may hold values from -3 to 3
- second_weight: bfloat16 [256, 3, 3, 128], P('chan'), may hold values from -0.1875 to 0.1875
- second_bias: float32 [256], P('chan'), may hold values from -3 to 3
Outputs:
- hidden: bfloat16 [1, 128, 128, 2048], P(None, 'chan', 'space')
- coarse: bfloat16 [1, 256, 64, 1024], P(None, 'chan', 'space')
Inputs may be any that keep to these rules, and one draw needn't show every extreme that they name: `top_map`: each entry of row s, column k is k - 1, k or k + 1 taken modulo 2048, or 2048 for a missing neighbour at a face corner; exactly 4 entries of each row equal 2048. `bottom_map`: each entry of row s, column k is k - 1, k or k + 1 taken modulo 2048, or 2048 for a missing neighbour at a face corner; exactly 4 entries of each row equal 2048.
All inputs are finite; a program needn't handle non-finite values.
Results may differ from a plain program's by a relative error of at most 0.012.
Values may be sent and summed in bfloat16 or wider, within the bound.
No kernel may reach another device: no remote copies, remote signals or barrier semaphores. Data moves between devices by JAX's collectives and lax.ppermute only.
A program may use at most 64 MiB of HBM per device.

v0:
```python
import jax
import jax.numpy as jnp
from jax import lax
from jax.sharding import PartitionSpec as P


def shifted(array, axis, by):
    devices = lax.axis_size(axis)
    pairs = [(i, i + by) for i in range(devices) if 0 <= i + by < devices]
    return lax.ppermute(array, axis, pairs)


def remap_window(source, table, first_col, width):
    cycle = table.shape[0]
    cols = (first_col + jnp.arange(width)) % cycle
    picked = lax.dynamic_slice_in_dim(
        jnp.concatenate([table, table], axis=0), first_col % cycle, width, axis=0
    )
    same = source[..., 1 : width + 1]
    prev = source[..., 0:width]
    nxt = source[..., 2 : width + 2]
    zero = jnp.zeros_like(same)
    out = jnp.where(picked == (cols + cycle - 1) % cycle, prev, zero)
    out = jnp.where(picked == (cols + 1) % cycle, nxt, out)
    out = jnp.where(picked == cols, same, out)
    return out


def remap_full(row, table):
    cycle = table.shape[0]
    wrapped = jnp.concatenate([row[..., -1:], row, row[..., :1]], axis=-1)
    return remap_window(wrapped, table, 0, cycle)


def conv(x, w, stride):
    return lax.conv_general_dilated(
        x,
        w,
        window_strides=stride,
        padding="VALID",
        dimension_numbers=("NCHW", "OHWI", "NCHW"),
        preferred_element_type=jnp.float32,
    )


def per_device(features, top_map, bottom_map, first_weight, first_bias, second_weight, second_bias):
    groups = lax.axis_size("chan")
    me = lax.axis_index("chan")
    x = features[0]
    rows = x.shape[1]
    cycle = x.shape[2]
    block = cycle // groups
    upper_map = top_map[0]
    lower_map = bottom_map[0]
    w1 = lax.all_gather(first_weight, "chan", axis=0, tiled=True)
    b1 = lax.all_gather(first_bias, "chan", axis=0, tiled=True)
    w2 = lax.all_gather(second_weight, "chan", axis=0, tiled=True)
    b2 = lax.all_gather(second_bias, "chan", axis=0, tiled=True)
    above_src = shifted(x[:, rows - 1, :], "space", 1)
    below_src = shifted(x[:, 0, :], "space", -1)
    above = remap_full(above_src, upper_map)
    below = remap_full(below_src, lower_map)
    padded = jnp.concatenate([above[:, None], x, below[:, None]], axis=1)
    halo = 3
    width = block + 2 * halo
    ext = jnp.concatenate([padded[..., cycle - halo :], padded, padded[..., :halo]], axis=-1)
    sends = jnp.stack([ext[..., j * block : j * block + width] for j in range(groups)], 0)
    got = lax.all_to_all(sends, "chan", 0, 0, tiled=True)
    window = got.reshape((-1,) + got.shape[2:])
    pre1 = conv(window[None], w1, (1, 1))
    hidden_win = jax.nn.gelu(pre1 + b1[None, :, None, None]).astype(jnp.bfloat16)[0]
    hidden_out = lax.all_to_all(
        hidden_win[:, :, halo - 1 : halo - 1 + block], "chan", 0, 2, tiled=True
    )
    rim_src = shifted(hidden_win[:, rows - 1, :], "space", 1)
    rim = remap_window(rim_src, upper_map, me * block - 1, block + 2)
    stacked = jnp.concatenate([rim[:, None], hidden_win[:, :, 1 : block + 3]], axis=1)
    pre2 = conv(stacked[None], w2, (1, 2))
    coarse_win = jax.nn.gelu(pre2 + b2[None, :, None, None]).astype(jnp.bfloat16)[0]
    coarse_out = lax.all_to_all(coarse_win, "chan", 0, 2, tiled=True)
    return (hidden_out[None], coarse_out[None])


def solution(mesh):
    placed = (
        P(None, "chan", "space", None),
        P("space", None),
        P("space", None),
        P("chan", None, None, None),
        P("chan"),
        P("chan", None, None, None),
        P("chan"),
    )
    return jax.shard_map(
        per_device,
        mesh=mesh,
        in_specs=placed,
        out_specs=(P(None, "chan", "space", None), P(None, "chan", "space", None)),
        check_vma=False,
    )
```

profile of v0, /device:TPU:64, one launch (start us, length us, event | category | flops | bytes accessed | tf_op | source)
XLA Modules:
  0.0 199.2 jit_solution(16435346475391124692)
XLA Ops:
  0.6 0.9 copy.98
  1.6 1.9 collective-permute-start
  3.5 5.8 %collective-permute-start.1 = (bf16[16,2048]{1,0:T(8,128)(2,1)S(1)}, bf16[16,2048]{1,0:T(8,128)(2,1)S(1)}, u32[]{:S(2)}, u32[]{:S(2)}) collective-permute-start(bf16[16,2048]{1,0:T(8,128)(2,1)S(1)} %get-tuple-element.15), channel_id=1, source_target_pairs={{8,0},{16,8},{24,16},{32,24},{40,32},{48,40},{56,48},{64,56},{72,6... | collective-permute-start | bytes 196616 | tf_op jit(solution)/shard_map/ppermute | solution.py:10
  9.3 0.7 copy-done.4
  10.0 1.3 dynamic-slice
  14.3 34.2 %all-reduce.2 = (f32[128]{0:T(128)S(1)}, f32[256]{0:T(256)S(1)}) all-reduce(f32[128]{0:T(128)S(1)} %dynamic-update-slice, f32[256]{0:T(256)S(1)} %dynamic-update-slice.1), channel_id=1, replica_groups=mesh['space'=64,'chan'=8] {'chan'}, use_global_device_ids=true, to_apply=%add | all-reduce | flops 384 | bytes 3072
  48.9 0.7 fusion.64
  49.6 0.7 fusion.61
  50.3 0.7 fusion.60
  51.0 0.7 fusion.59
  51.7 0.7 fusion.58
  52.4 0.7 fusion.57
  53.1 0.7 fusion.56
  53.8 0.7 fusion.55
  54.6 3.6 %all-to-all-start = ((bf16[8,16,4,262]{3,1,2,0:T(8,128)(2,1)}), bf16[8,16,4,262]{3,1,2,0:T(8,128)(2,1)S(1)}, u32[]{:S(2)}, u32[]{:S(2)}) async-start(bf16[8,16,4,262]{3,1,2,0:T(8,128)(2,1)} %fusion.55), calls=%async_computation | async-start | bytes 786432 | tf_op jit(solution)/shard_map/all_to_all | solution.py:68
  58.2 49.5 %all_gather.12 = bf16[128,3,3,128]{3,0,2,1:T(8,128)(2,1)S(1)} all-gather(bf16[16,3,3,128]{3,0,2,1:T(8,128)(2,1)S(1)} %copy-done.2), channel_id=1, replica_groups=mesh['space'=64,'chan'=8] {'chan'}, dimensions={0}, use_global_device_ids=true | all-gather | bytes 331776 | tf_op jit(solution)/shard_map/all_gather | solution.py:55
  107.8 46.5 %all_gather.14 = bf16[256,3,3,128]{3,0,2,1:T(8,128)(2,1)S(1)} all-gather(bf16[32,3,3,128]{3,0,2,1:T(8,128)(2,1)S(1)} %copy-done.1), channel_id=1, replica_groups=mesh['space'=64,'chan'=8] {'chan'}, dimensions={0}, use_global_device_ids=true | all-gather | bytes 663552 | tf_op jit(solution)/shard_map/all_gather | solution.py:57
  154.7 0.7 copy-done.7
  156.4 1.9 collective-permute-start.2
  158.3 5.8 %collective-permute-done.2 = bf16[128,260]{0,1:T(8,128)(2,1)S(1)} collective-permute-done((bf16[128,260]{0,1:T(8,128)(2,1)S(1)}, bf16[128,260]{0,1:T(8,128)(2,1)S(1)}, u32[]{:S(2)}, u32[]{:S(2)}) %collective-permute-start.2) | collective-permute-done | bytes 66592 | tf_op jit(solution)/shard_map/ppermute | solution.py:10
  164.4 0.8 slice-done
  165.6 0.7 copy-done.8
  167.3 0.7 reduce
  168.1 0.7 reshape.47
  168.7 5.3 %all-to-all-start.2 = ((bf16[8,2,2048]{2,1,0:T(2,128)(2,1)}), bf16[8,2,2048]{2,1,0:T(2,128)(2,1)S(1)}, u32[]{:S(2)}, u32[]{:S(2)}) async-start(bf16[8,2,2048]{2,1,0:T(2,128)(2,1)} %reshape.47), calls=%async_computation.2 | async-start | bytes 131072 | tf_op jit(solution)/shard_map/all_to_all | solution.py:80
  174.1 0.9 slice-done.1
  175.0 0.8 copy.78
  175.8 8.8 %all-to-all-done.2 = bf16[8,2,2048]{2,1,0:T(2,128)(2,1)S(1)} async-done(((bf16[8,2,2048]{2,1,0:T(2,128)(2,1)}), bf16[8,2,2048]{2,1,0:T(2,128)(2,1)S(1)}, u32[]{:S(2)}, u32[]{:S(2)}) %all-to-all-start.2) | async-done | bytes 65568 | tf_op jit(solution)/shard_map/all_to_all | solution.py:80
  184.6 3.4 %all-to-all-start.1 = ((bf16[128,2,256]{2,1,0:T(2,128)(2,1)}), bf16[128,2,256]{2,1,0:T(2,128)(2,1)S(1)}, u32[]{:S(2)}, u32[]{:S(2)}) async-start(bf16[128,2,256]{2,1,0:T(2,128)(2,1)} %copy.78), calls=%async_computation.1 | async-start | bytes 262144 | tf_op jit(solution)/shard_map/all_to_all | solution.py:72
  188.1 0.7 broadcast_in_dim.67
  188.7 9.7 %all-to-all-done.1 = bf16[128,2,256]{2,1,0:T(2,128)(2,1)S(1)} async-done(((bf16[128,2,256]{2,1,0:T(2,128)(2,1)}), bf16[128,2,256]{2,1,0:T(2,128)(2,1)S(1)}, u32[]{:S(2)}, u32[]{:S(2)}) %all-to-all-start.1) | async-done | bytes 131104 | tf_op jit(solution)/shard_map/all_to_all | solution.py:72
  198.5 0.7 reshape.46
  (61 shorter events, 5.5 us)
Async XLA Ops:
  1.6 7.7 %copy-start.3 = (s32[1,2048]{1,0:T(1,128)S(1)}, s32[1,2048]{1,0:T(1,128)}, u32[]{:S(2)}) copy-start(s32[1,2048]{1,0:T(1,128)} %param.8) | copy-start | bytes 24580
  1.6 46.9 %collective-permute-start = (bf16[16,2048]{1,0:T(8,128)(2,1)S(1)}, bf16[16,2048]{1,0:T(8,128)(2,1)S(1)}, u32[]{:S(2)}, u32[]{:S(2)}) collective-permute-start(bf16[16,2048]{1,0:T(8,128)(2,1)S(1)} %get-tuple-element.14), channel_id=1, source_target_pairs={{0,8},{8,16},{16,24},{24,32},{32,40},{40,48},{48,56},{56,64},{64,7... | collective-permute-start | bytes 196616 | tf_op jit(solution)/shard_map/ppermute | solution.py:10
  3.5 45.0 %collective-permute-start.1 = (bf16[16,2048]{1,0:T(8,128)(2,1)S(1)}, bf16[16,2048]{1,0:T(8,128)(2,1)S(1)}, u32[]{:S(2)}, u32[]{:S(2)}) collective-permute-start(bf16[16,2048]{1,0:T(8,128)(2,1)S(1)} %get-tuple-element.15), channel_id=1, source_target_pairs={{8,0},{16,8},{24,16},{32,24},{40,32},{48,40},{56,48},{64,56},{72,6... | collective-permute-start | bytes 196616 | tf_op jit(solution)/shard_map/ppermute | solution.py:10
  9.3 0.7 copy-start.4
  12.6 0.7 copy-start.5
  13.5 0.7 copy-start.6
  54.5 3.7 %copy-start.2 = (bf16[16,3,3,128]{3,0,2,1:T(8,128)(2,1)S(1)}, bf16[16,3,3,128]{3,0,2,1:T(8,128)(2,1)}, u32[]{:S(2)}) copy-start(bf16[16,3,3,128]{3,0,2,1:T(8,128)(2,1)} %param.10) | copy-start | bytes 110596
  54.6 99.7 %all-to-all-start = ((bf16[8,16,4,262]{3,1,2,0:T(8,128)(2,1)}), bf16[8,16,4,262]{3,1,2,0:T(8,128)(2,1)S(1)}, u32[]{:S(2)}, u32[]{:S(2)}) async-start(bf16[8,16,4,262]{3,1,2,0:T(8,128)(2,1)} %fusion.55), calls=%async_computation | async-start | bytes 786432 | tf_op jit(solution)/shard_map/all_to_all | solution.py:68
  58.2 49.5 %copy-start.1 = (bf16[32,3,3,128]{3,0,2,1:T(8,128)(2,1)S(1)}, bf16[32,3,3,128]{3,0,2,1:T(8,128)(2,1)}, u32[]{:S(2)}) copy-start(bf16[32,3,3,128]{3,0,2,1:T(8,128)(2,1)} %param.12) | copy-start | bytes 221188
  154.7 0.7 copy-start.7
  156.2 2.1 %copy-start = (bf16[128,2,260]{0,1,2:T(2,128)(2,1)}, bf16[128,2,260]{0,1,2:T(2,128)(2,1)S(1)}, u32[]{:S(2)}) copy-start(bf16[128,2,260]{0,1,2:T(2,128)(2,1)S(1)} %slice_bitcast_fusion) | copy-start | bytes 399364
  156.4 7.7 %collective-permute-start.2 = (bf16[128,260]{0,1:T(8,128)(2,1)S(1)}, bf16[128,260]{0,1:T(8,128)(2,1)S(1)}, u32[]{:S(2)}, u32[]{:S(2)}) collective-permute-start(bf16[128,260]{0,1:T(8,128)(2,1)S(1)} %bitcast.104), channel_id=1, source_target_pairs={{0,8},{8,16},{16,24},{24,32},{32,40},{40,48},{48,56},{56,64},{64,7... | collective-permute-start | bytes 199688 | tf_op jit(solution)/shard_map/ppermute | solution.py:10
  164.3 0.9 slice-start
  165.6 0.7 copy-start.8
  168.7 15.8 %all-to-all-start.2 = ((bf16[8,2,2048]{2,1,0:T(2,128)(2,1)}), bf16[8,2,2048]{2,1,0:T(2,128)(2,1)S(1)}, u32[]{:S(2)}, u32[]{:S(2)}) async-start(bf16[8,2,2048]{2,1,0:T(2,128)(2,1)} %reshape.47), calls=%async_computation.2 | async-start | bytes 131072 | tf_op jit(solution)/shard_map/all_to_all | solution.py:80
  174.1 0.9 slice-start.1
  184.6 13.9 %all-to-all-start.1 = ((bf16[128,2,256]{2,1,0:T(2,128)(2,1)}), bf16[128,2,256]{2,1,0:T(2,128)(2,1)S(1)}, u32[]{:S(2)}, u32[]{:S(2)}) async-start(bf16[128,2,256]{2,1,0:T(2,128)(2,1)} %copy.78), calls=%async_computation.1 | async-start | bytes 262144 | tf_op jit(solution)/shard_map/all_to_all | solution.py:72
where the time goes:
time: 200 us; the launch traced here: 199 us
  blocking collectives  130 us (65%)
  waiting for transfers between devices  24.3 us (12%)
  starting transfers between devices  21.9 us (11%)
  local copies, waits for them, and re-layouts  16.6 us (8%)
  other arithmetic  2.91 us (1%)
  between operations  2.33 us (1%)
    all_gather x1, blocking collectives, per_device(): w1 = lax.all_gather(first_weight, 'chan', axis=0, tiled=True)  49.5 us
    all_gather x1, blocking collectives, per_device(): w2 = lax.all_gather(second_weight, 'chan', axis=0, tiled=True)  46.5 us
    unnamed x1, blocking collectives  34.2 us
    unnamed x38, local copies, waits for them, and re-layouts  11.9 us
    all_to_all x1, waiting for transfers between devices, per_device(): lax.all_to_all(hidden_win[:, :, halo - 1:halo - 1 + block], 'chan', 0, 2,...  9.74 us
    ppermute x3, starting transfers between devices, shifted(): return lax.ppermute(array, axis, pairs)  9.59 us
    all_to_all x1, waiting for transfers between devices, per_device(): coarse_out = lax.all_to_all(coarse_win, 'chan', 0, 2, tiled=True)  8.79 us
    ppermute x3, waiting for transfers between devices, shifted(): return lax.ppermute(array, axis, pairs)  5.76 us
  transfers between devices with their start and end apart: 6, of which 3 were waited for; matrix products, arithmetic and copies ran while one was open for 2% of the time, Pallas kernels for 0%

commit v1 on v0

--- a/solution.py
+++ b/solution.py
@@ -52,7 +52,9 @@
     block = cycle // groups
     upper_map = top_map[0]
     lower_map = bottom_map[0]
-    w1 = lax.all_gather(first_weight, "chan", axis=0, tiled=True)
+    w1 = jnp.concatenate(
+        lax.all_to_all(jnp.stack([first_weight] * lax.axis_size("chan")), "chan", 0, 0), axis=0
+    )
     b1 = lax.all_gather(first_bias, "chan", axis=0, tiled=True)
     w2 = lax.all_gather(second_weight, "chan", axis=0, tiled=True)
     b2 = lax.all_gather(second_bias, "chan", axis=0, tiled=True)

time: 200 us -> 167 us (0.83)
  blocking collectives: 130 us -> 77.5 us
  starting transfers between devices: 21.9 us -> 37.7 us
  waiting for transfers between devices: 24.3 us -> 28.7 us
    all_gather x1 -> x0, blocking collectives: 49.5 us -> none  [per_device(): w1 = lax.all_gather(first_weight, 'chan', axis=0, tiled=True)]
    all_to_all x0 -> x1, starting transfers between devices: none -> 12 us  [per_device(): lax.all_to_all(jnp.stack([first_weight] * lax.axis_size('chan')), 'chan',...]
    all_to_all x0 -> x1, waiting for transfers between devices: none -> 4.6 us  [per_device(): lax.all_to_all(jnp.stack([first_weight] * lax.axis_size('chan')), 'chan',...]
    unnamed x1, blocking collectives: 34.2 us -> 31.8 us
    all_to_all x1, starting transfers between devices: 5.35 us -> 7.65 us  [per_device(): coarse_out = lax.all_to_all(coarse_win, 'chan', 0, 2, tiled=True)]
  transfers between devices with their start and end apart: 6 -> 7, of which waited for: 3 -> 4; matrix products, arithmetic and copies ran while one was open for 2% -> 6% of each run, Pallas kernels for 0% -> 0%
where the time goes in v1:
time: 167 us; the launch traced here: 166 us
  blocking collectives  77.5 us (46%)
  starting transfers between devices  37.7 us (23%)
  waiting for transfers between devices  28.7 us (17%)
  local copies, waits for them, and re-layouts  16.3 us (10%)
  other arithmetic  2.9 us (2%)
  between operations  2.35 us (1%)
    all_gather x1, blocking collectives, per_device(): w2 = lax.all_gather(second_weight, 'chan', axis=0, tiled=True)  45.7 us
    unnamed x1, blocking collectives  31.8 us
    all_to_all x1, starting transfers between devices, per_device(): lax.all_to_all(jnp.stack([first_weight] * lax.axis_size('chan')), 'chan',...  12 us
    unnamed x38, local copies, waits for them, and re-layouts  10.8 us
    all_to_all x1, waiting for transfers between devices, per_device(): lax.all_to_all(hidden_win[:, :, halo - 1:halo - 1 + block], 'chan', 0, 2,...  9.74 us
    ppermute x3, starting transfers between devices, shifted(): return lax.ppermute(array, axis, pairs)  9.59 us
    all_to_all x1, waiting for transfers between devices, per_device(): coarse_out = lax.all_to_all(coarse_win, 'chan', 0, 2, tiled=True)  8.56 us
    all_to_all x1, starting transfers between devices, per_device(): coarse_out = lax.all_to_all(coarse_win, 'chan', 0, 2, tiled=True)  7.65 us
  transfers between devices with their start and end apart: 7, of which 4 were waited for; matrix products, arithmetic and copies ran while one was open for 6% of the time, Pallas kernels for 0%

profile of v1, /device:TPU:64, one launch (start us, length us, event | category | flops | bytes accessed | tf_op | source)
XLA Modules:
  0.0 166.3 jit_solution(11377209908714645235)
XLA Ops:
  0.6 0.9 copy.100
  1.6 1.9 %collective-permute-start = (bf16[16,2048]{1,0:T(8,128)(2,1)S(1)}, bf16[16,2048]{1,0:T(8,128)(2,1)S(1)}, u32[]{:S(2)}, u32[]{:S(2)}) collective-permute-start(bf16[16,2048]{1,0:T(8,128)(2,1)S(1)} %get-tuple-element.14), channel_id=1, source_target_pairs={{0,8},{8,16},{16,24},{24,32},{32,40},{40,48},{48,56},{56,64},{64,7... | collective-permute-start | bytes 196616 | tf_op jit(solution)/shard_map/ppermute | solution.py:10
  3.5 5.8 %collective-permute-start.1 = (bf16[16,2048]{1,0:T(8,128)(2,1)S(1)}, bf16[16,2048]{1,0:T(8,128)(2,1)S(1)}, u32[]{:S(2)}, u32[]{:S(2)}) collective-permute-start(bf16[16,2048]{1,0:T(8,128)(2,1)S(1)} %get-tuple-element.15), channel_id=1, source_target_pairs={{8,0},{16,8},{24,16},{32,24},{40,32},{48,40},{56,48},{64,56},{72,6... | collective-permute-start | bytes 196616 | tf_op jit(solution)/shard_map/ppermute | solution.py:10
  9.3 0.8 stack.47
  10.1 12.0 %all-to-all-start.1 = ((bf16[8,16,3,3,128]{4,1,3,2,0:T(8,128)(2,1)}), bf16[8,16,3,3,128]{4,1,3,2,0:T(8,128)(2,1)S(1)}, u32[]{:S(2)}, u32[]{:S(2)}) async-start(bf16[8,16,3,3,128]{4,1,3,2,0:T(8,128)(2,1)} %stack.47), calls=%async_computation.1 | async-start | bytes 589824 | tf_op jit(solution)/shard_map/all_to_all | solution.py:56
  22.1 0.7 copy-done.4
  23.2 0.7 fusion.64
  23.9 0.7 fusion.61
  24.6 0.7 fusion.60
  25.3 0.7 fusion.59
  26.0 0.7 fusion.58
  26.7 0.7 fusion.57
  27.4 0.7 fusion.56
  28.1 0.7 fusion.55
  28.8 4.6 %all-to-all-done.1 = bf16[8,16,3,3,128]{4,1,3,2,0:T(8,128)(2,1)S(1)} async-done(((bf16[8,16,3,3,128]{4,1,3,2,0:T(8,128)(2,1)}), bf16[8,16,3,3,128]{4,1,3,2,0:T(8,128)(2,1)S(1)}, u32[]{:S(2)}, u32[]{:S(2)}) %all-to-all-start.1) | async-done | bytes 294944 | tf_op jit(solution)/shard_map/all_to_all | solution.py:56
  33.4 5.1 %all-to-all-start = ((bf16[8,16,4,262]{3,1,2,0:T(8,128)(2,1)}), bf16[8,16,4,262]{3,1,2,0:T(8,128)(2,1)S(1)}, u32[]{:S(2)}, u32[]{:S(2)}) async-start(bf16[8,16,4,262]{3,1,2,0:T(8,128)(2,1)} %fusion.55), calls=%async_computation | async-start | bytes 786432 | tf_op jit(solution)/shard_map/all_to_all | solution.py:70
  38.6 1.3 dynamic-slice
  41.7 31.8 %all-reduce.2 = (f32[128]{0:T(128)S(1)}, f32[256]{0:T(256)S(1)}) all-reduce(f32[128]{0:T(128)S(1)} %dynamic-update-slice, f32[256]{0:T(256)S(1)} %dynamic-update-slice.1), channel_id=1, replica_groups=mesh['space'=64,'chan'=8] {'chan'}, use_global_device_ids=true, to_apply=%add | all-reduce | flops 384 | bytes 3072
  73.6 45.7 %all_gather.10 = bf16[256,3,3,128]{3,0,2,1:T(8,128)(2,1)S(1)} all-gather(bf16[32,3,3,128]{3,0,2,1:T(8,128)(2,1)S(1)} %copy-done.1), channel_id=1, replica_groups=mesh['space'=64,'chan'=8] {'chan'}, dimensions={0}, use_global_device_ids=true | all-gather | bytes 663552 | tf_op jit(solution)/shard_map/all_gather | solution.py:59
  119.8 0.7 copy-done.7
  121.4 1.9 %collective-permute-start.2 = (bf16[128,260]{0,1:T(8,128)(2,1)S(1)}, bf16[128,260]{0,1:T(8,128)(2,1)S(1)}, u32[]{:S(2)}, u32[]{:S(2)}) collective-permute-start(bf16[128,260]{0,1:T(8,128)(2,1)S(1)} %bitcast.106), channel_id=1, source_target_pairs={{0,8},{8,16},{16,24},{24,32},{32,40},{40,48},{48,56},{56,64},{64,7... | collective-permute-start | bytes 199688 | tf_op jit(solution)/shard_map/ppermute | solution.py:10
  123.4 5.8 %collective-permute-done.2 = bf16[128,260]{0,1:T(8,128)(2,1)S(1)} collective-permute-done((bf16[128,260]{0,1:T(8,128)(2,1)S(1)}, bf16[128,260]{0,1:T(8,128)(2,1)S(1)}, u32[]{:S(2)}, u32[]{:S(2)}) %collective-permute-start.2) | collective-permute-done | bytes 66592 | tf_op jit(solution)/shard_map/ppermute | solution.py:10
  129.4 0.8 slice-done
  130.7 0.7 copy-done.8
  133.8 7.6 %all-to-all-start.3 = ((bf16[8,2,2048]{2,1,0:T(2,128)(2,1)}), bf16[8,2,2048]{2,1,0:T(2,128)(2,1)S(1)}, u32[]{:S(2)}, u32[]{:S(2)}) async-start(bf16[8,2,2048]{2,1,0:T(2,128)(2,1)} %reshape.53), calls=%async_computation.3 | async-start | bytes 131072 | tf_op jit(solution)/shard_map/all_to_all | solution.py:82
  141.4 0.9 slice-done.1
  142.3 0.8 copy.80
  143.1 8.6 %all-to-all-done.3 = bf16[8,2,2048]{2,1,0:T(2,128)(2,1)S(1)} async-done(((bf16[8,2,2048]{2,1,0:T(2,128)(2,1)}), bf16[8,2,2048]{2,1,0:T(2,128)(2,1)S(1)}, u32[]{:S(2)}, u32[]{:S(2)}) %all-to-all-start.3) | async-done | bytes 65568 | tf_op jit(solution)/shard_map/all_to_all | solution.py:82
  151.7 3.4 %all-to-all-start.2 = ((bf16[128,2,256]{2,1,0:T(2,128)(2,1)}), bf16[128,2,256]{2,1,0:T(2,128)(2,1)S(1)}, u32[]{:S(2)}, u32[]{:S(2)}) async-start(bf16[128,2,256]{2,1,0:T(2,128)(2,1)} %copy.80), calls=%async_computation.2 | async-start | bytes 262144 | tf_op jit(solution)/shard_map/all_to_all | solution.py:74
  155.2 0.7 broadcast_in_dim.67
  155.8 9.7 %all-to-all-done.2 = bf16[128,2,256]{2,1,0:T(2,128)(2,1)S(1)} async-done(((bf16[128,2,256]{2,1,0:T(2,128)(2,1)}), bf16[128,2,256]{2,1,0:T(2,128)(2,1)S(1)}, u32[]{:S(2)}, u32[]{:S(2)}) %all-to-all-start.2) | async-done | bytes 131104 | tf_op jit(solution)/shard_map/all_to_all | solution.py:74
  165.6 0.7 reshape.52
  (64 shorter events, 5.7 us)
Async XLA Ops:
  1.6 7.7 %copy-start.2 = (bf16[16,3,3,128]{3,0,2,1:T(8,128)(2,1)S(1)}, bf16[16,3,3,128]{3,0,2,1:T(8,128)(2,1)}, u32[]{:S(2)}) copy-start(bf16[16,3,3,128]{3,0,2,1:T(8,128)(2,1)} %param.10) | copy-start | bytes 110596
  1.6 21.1 %collective-permute-start = (bf16[16,2048]{1,0:T(8,128)(2,1)S(1)}, bf16[16,2048]{1,0:T(8,128)(2,1)S(1)}, u32[]{:S(2)}, u32[]{:S(2)}) collective-permute-start(bf16[16,2048]{1,0:T(8,128)(2,1)S(1)} %get-tuple-element.14), channel_id=1, source_target_pairs={{0,8},{8,16},{16,24},{24,32},{32,40},{40,48},{48,56},{56,64},{64,7... | collective-permute-start | bytes 196616 | tf_op jit(solution)/shard_map/ppermute | solution.py:10
  3.5 19.3 %collective-permute-start.1 = (bf16[16,2048]{1,0:T(8,128)(2,1)S(1)}, bf16[16,2048]{1,0:T(8,128)(2,1)S(1)}, u32[]{:S(2)}, u32[]{:S(2)}) collective-permute-start(bf16[16,2048]{1,0:T(8,128)(2,1)S(1)} %get-tuple-element.15), channel_id=1, source_target_pairs={{8,0},{16,8},{24,16},{32,24},{40,32},{48,40},{56,48},{64,56},{72,6... | collective-permute-start | bytes 196616 | tf_op jit(solution)/shard_map/ppermute | solution.py:10
  10.1 12.0 %copy-start.3 = (s32[1,2048]{1,0:T(1,128)S(1)}, s32[1,2048]{1,0:T(1,128)}, u32[]{:S(2)}) copy-start(s32[1,2048]{1,0:T(1,128)} %param.8) | copy-start | bytes 24580
  10.1 23.3 %all-to-all-start.1 = ((bf16[8,16,3,3,128]{4,1,3,2,0:T(8,128)(2,1)}), bf16[8,16,3,3,128]{4,1,3,2,0:T(8,128)(2,1)S(1)}, u32[]{:S(2)}, u32[]{:S(2)}) async-start(bf16[8,16,3,3,128]{4,1,3,2,0:T(8,128)(2,1)} %stack.47), calls=%async_computation.1 | async-start | bytes 589824 | tf_op jit(solution)/shard_map/all_to_all | solution.py:56
  22.0 0.7 copy-start.4
  33.4 7.8 %copy-start.5 = (f32[32]{0:T(128)S(1)}, f32[32]{0:T(128)}, u32[]{:S(2)}) copy-start(f32[32]{0:T(128)} %param.13) | copy-start | bytes 388
  33.4 8.0 %copy-start.6 = (f32[16]{0:T(128)S(1)}, f32[16]{0:T(128)}, u32[]{:S(2)}) copy-start(f32[16]{0:T(128)} %param.11) | copy-start | bytes 196
  33.4 85.9 %all-to-all-start = ((bf16[8,16,4,262]{3,1,2,0:T(8,128)(2,1)}), bf16[8,16,4,262]{3,1,2,0:T(8,128)(2,1)S(1)}, u32[]{:S(2)}, u32[]{:S(2)}) async-start(bf16[8,16,4,262]{3,1,2,0:T(8,128)(2,1)} %fusion.55), calls=%async_computation | async-start | bytes 786432 | tf_op jit(solution)/shard_map/all_to_all | solution.py:70
  38.6 35.1 %copy-start.1 = (bf16[32,3,3,128]{3,0,2,1:T(8,128)(2,1)S(1)}, bf16[32,3,3,128]{3,0,2,1:T(8,128)(2,1)}, u32[]{:S(2)}) copy-start(bf16[32,3,3,128]{3,0,2,1:T(8,128)(2,1)} %param.12) | copy-start | bytes 221188
  119.8 0.7 copy-start.7
  121.2 2.1 %copy-start = (bf16[128,2,260]{0,1,2:T(2,128)(2,1)}, bf16[128,2,260]{0,1,2:T(2,128)(2,1)S(1)}, u32[]{:S(2)}) copy-start(bf16[128,2,260]{0,1,2:T(2,128)(2,1)S(1)} %slice_bitcast_fusion) | copy-start | bytes 399364
  121.4 7.7 %collective-permute-start.2 = (bf16[128,260]{0,1:T(8,128)(2,1)S(1)}, bf16[128,260]{0,1:T(8,128)(2,1)S(1)}, u32[]{:S(2)}, u32[]{:S(2)}) collective-permute-start(bf16[128,260]{0,1:T(8,128)(2,1)S(1)} %bitcast.106), channel_id=1, source_target_pairs={{0,8},{8,16},{16,24},{24,32},{32,40},{40,48},{48,56},{56,64},{64,7... | collective-permute-start | bytes 199688 | tf_op jit(solution)/shard_map/ppermute | solution.py:10
  129.3 0.9 slice-start
  130.6 0.7 copy-start.8
  133.8 17.9 %all-to-all-start.3 = ((bf16[8,2,2048]{2,1,0:T(2,128)(2,1)}), bf16[8,2,2048]{2,1,0:T(2,128)(2,1)S(1)}, u32[]{:S(2)}, u32[]{:S(2)}) async-start(bf16[8,2,2048]{2,1,0:T(2,128)(2,1)} %reshape.53), calls=%async_computation.3 | async-start | bytes 131072 | tf_op jit(solution)/shard_map/all_to_all | solution.py:82
  141.4 0.9 slice-start.1
  151.7 13.9 %all-to-all-start.2 = ((bf16[128,2,256]{2,1,0:T(2,128)(2,1)}), bf16[128,2,256]{2,1,0:T(2,128)(2,1)S(1)}, u32[]{:S(2)}, u32[]{:S(2)}) async-start(bf16[128,2,256]{2,1,0:T(2,128)(2,1)} %copy.80), calls=%async_computation.2 | async-start | bytes 262144 | tf_op jit(solution)/shard_map/all_to_all | solution.py:74
